TPU v7x, 256 devices: a whole 4x4x8 slice. The times are simulated.
256 devices in a mesh: prow: 64 (over x, z, core), pcol: 4 (over y).
Axes of the slice: x: 4, y: 4, z: 8, core: 2. Of those that a mesh axis runs over, the one named last changes fastest.
Arguments:
- right_side: float32 [512, 65536], P('pcol', 'prow'), may hold values from -6 to 6
- factor: float32 [65536, 2048], P('prow', 'pcol'), may hold values from -0.125 to 0.125
- inverses: float32 [2048, 512], replicated, as said below
Outputs:
- solved: float32 [512, 65536], P('pcol', 'prow')
Inputs may be any that keep to these rules, and one draw needn't show every extreme that they name: Each 512 x 512 block of inverses is lower triangular with a positive diagonal.
All inputs are finite; a program needn't handle non-finite values.
Results may differ from a plain program's by a relative error of at most 0.0001.
Values sent between devices are 32-bit elements; how exact they have to be, the bound alone decides.
No kernel may reach another device: no remote copies, remote signals or barrier semaphores. Data moves between devices by JAX's collectives and lax.ppermute only.
A program may use at most 64 MiB of HBM per device.

v0:
```python
import jax
import jax.numpy as jnp
from jax import lax
from jax.sharding import PartitionSpec as P


def contract(left, right):
    return lax.dot_general(
        left,
        right,
        (((1,), (1,)), ((), ())),
        precision=lax.Precision.HIGHEST,
        preferred_element_type=jnp.float32,
    )


AXES = ("prow", "pcol")


def per_device(right_side, factor, inverses):
    block = factor.shape[1]
    rhs_width = right_side.shape[0]
    n_col = lax.axis_size("pcol")
    n_row = lax.axis_size("prow")
    steps = n_col
    row_at = lax.axis_index("prow")
    col_at = lax.axis_index("pcol")

    def at(p, c):
        return p * n_col + c

    top_rhs = right_side[:, :block]
    first_rhs = top_rhs
    for i in range(1, steps):
        pairs = [(at(0, c), at(i, c)) for c in range(n_col)]
        first_rhs = jnp.where(row_at == i, lax.ppermute(top_rhs, AXES, pairs), first_rhs)
    first_rhs, first_rows = lax.optimization_barrier((first_rhs, factor[:block]))
    lower_first = lax.all_gather(first_rows, "pcol", axis=1, tiled=True)
    second_rows, _ = lax.optimization_barrier((factor[block:], lower_first))
    lower_second = lax.all_gather(second_rows, "pcol", axis=1, tiled=True)
    acc = jnp.zeros((rhs_width, block), jnp.float32)
    own = jnp.zeros((rhs_width, block), jnp.float32)
    for k in range(steps):
        if k == 0:
            solved = contract(first_rhs, inverses[:block])
        else:
            solved = contract(top_rhs - acc, inverses[k * block : (k + 1) * block])
        own = jnp.where(row_at == k, solved, own)
        if k == steps - 2:
            own_early = own
        if k == steps - 1:
            break
        if k == 0:
            arrived = solved
        else:
            arrived = jnp.zeros_like(solved)
            for i in range(k + 1, steps):
                pairs = [(at(k, c), at(i, c)) for c in range(n_col)]
                arrived = arrived + lax.ppermute(solved, AXES, pairs)
        acc = acc + contract(arrived, lower_first[:, k * block : (k + 1) * block])
    fan_z = min(steps, n_row // steps)
    stride_x = steps * fan_z
    spread = []
    for piece, sources in ((own_early, range(steps - 1)), (own, (steps - 1,))):
        for stride, fan in ((stride_x, n_row // stride_x), (steps, fan_z)):
            holders = [p for p in range(n_row) if p % (stride * fan) in sources]
            received = piece
            for hop in sorted(range(1, fan), key=lambda h: -min(h, fan - h)):
                pairs = [(p, p + hop * stride) for p in holders]
                arrived = lax.ppermute(piece, "prow", pairs)
                received = jnp.where(row_at % (stride * fan) // stride == hop, arrived, received)
            piece = jnp.where(row_at % stride < steps, received, piece)
        spread.append(piece)
    piece = jnp.where(row_at % steps == steps - 1, spread[1], spread[0])
    b0 = row_at % 2
    b1 = row_at // 2 % 2
    other = lax.ppermute(piece, "prow", [(p, p ^ 2) for p in range(n_row)])
    pair = jnp.where(
        b1 == 0, jnp.concatenate([piece, other], axis=1), jnp.concatenate([other, piece], axis=1)
    )
    theirs = lax.ppermute(pair, "prow", [(p, p ^ 1) for p in range(n_row)])
    mine, yours = ((pair[:, :block], pair[:, block:]), (theirs[:, :block], theirs[:, block:]))
    mine_first = jnp.concatenate([mine[0], yours[0], mine[1], yours[1]], axis=1)
    theirs_first = jnp.concatenate([yours[0], mine[0], yours[1], mine[1]], axis=1)
    panel = jnp.where(b0 == 0, mine_first, theirs_first)
    second = right_side[:, block:] - contract(panel, lower_second)
    first = right_side[:, :block] - contract(panel, lower_first)
    head_block = jnp.where(row_at < steps, own, first)
    return jnp.concatenate([head_block, second], axis=1)


def solution(mesh):
    return jax.shard_map(
        per_device,
        mesh=mesh,
        in_specs=(P("pcol", "prow"), P("prow", "pcol"), P()),
        out_specs=P("pcol", "prow"),
        check_vma=False,
    )
```

profile of v0, /device:TPU:1, one launch (start us, length us, event | category | flops | bytes accessed | tf_op | source)
XLA Modules:
  0.0 148.4 jit_solution(318537297239091147)
XLA Ops:
  6.5 0.0 copy-start
  6.5 0.0 all-gather.3.cloned.1.call-start
  6.5 1.0 slice.46
  7.6 0.7 collective-permute-start
  8.3 0.7 collective-permute-start.1
  8.9 1.3 collective-permute-start.2
  10.3 3.2 %fusion.20 = (f32[512,512]{1,0:T(8,128)}, f32[512,512]{1,0:T(8,128)}) fusion(f32[1024,512]{1,0:T(8,128)} %param.4), kind=kLoop, calls=%fused_computation.33 | loop fusion | bytes 4194304 | tf_op jit(solution)/shard_map/slice | solution.py:37
  13.4 0.0 collective-permute-done
  13.4 0.0 collective-permute-done.1
  13.4 2.6 %collective-permute-done.2 = f32[128,512]{1,0:T(8,128)S(1)} collective-permute-done((f32[128,512]{1,0:T(8,128)S(1)}, f32[128,512]{1,0:T(8,128)S(1)}, u32[]{:S(2)}, u32[]{:S(2)}) %collective-permute-start.2) | collective-permute-done | bytes 262176 | tf_op jit(solution)/shard_map/ppermute | solution.py:36
  16.0 0.0 copy-done
  16.0 0.1 select_select_fusion.4
  16.1 0.0 all-gather.3.cloned.1.call-update
  16.1 0.0 all-gather.5.cloned.1.call-start
  16.2 51.6 %all-gather.3.cloned.1.call-done = f32[512,2048]{1,0:T(8,128)} async-done(((f32[512,512]{1,0:T(8,128)}), f32[512,2048]{1,0:T(8,128)}) %all-gather.3.cloned.1.call-update) | async-done | bytes 4194320 | tf_op jit(solution)/shard_map/all_gather | solution.py:38
  67.7 0.0 all-gather.5.cloned.1.call-update
  67.7 2.4 %fusion.11 = f32[128,512]{1,0:T(8,128)S(1)} fusion(f32[128,512]{1,0:T(8,128)S(1)} %select_select_fusion.4, f32[2048,512]{1,0:T(8,128)} %param.5), kind=kOutput, calls=%fused_computation.17 | convolution fusion | flops 402653184 | bytes 1572864 | tf_op jit(solution)/shard_map/dot_general | solution.py:8
  70.1 2.4 %fusion.4 = f32[128,512]{1,0:T(8,128)S(1)} fusion(f32[128,512]{1,0:T(8,128)S(1)} %fusion.11, f32[512,2048]{1,0:T(8,128)} %all-gather.3.cloned.1.call-done), kind=kOutput, calls=%fused_computation.9 | convolution fusion | flops 402653184 | bytes 1572864 | tf_op jit(solution)/shard_map/dot_general | solution.py:8
  72.5 2.4 %fusion.9 = f32[128,512]{1,0:T(8,128)S(1)} fusion(f32[2048,512]{1,0:T(8,128)} %param.5, f32[128,512]{1,0:T(8,128)S(1)} %fusion.4, f32[128,1024]{1,0:T(8,128)S(1)} %copy-done), kind=kOutput, calls=%fused_computation.15 | convolution fusion | flops 402718720 | bytes 1835008 | tf_op jit(solution)/shard_map/dot_general | solution.py:8
  74.9 3.8 %collective-permute-start.3 = (f32[128,512]{1,0:T(8,128)S(1)}, f32[128,512]{1,0:T(8,128)S(1)}, u32[]{:S(2)}, u32[]{:S(2)}) collective-permute-start(f32[128,512]{1,0:T(8,128)S(1)} %fusion.9), channel_id=1, source_target_pairs={{4,8},{5,9},{6,10},{7,11}} | collective-permute-start | bytes 786440 | tf_op jit(solution)/shard_map/ppermute | solution.py:59
  78.7 1.3 collective-permute-start.4
  80.0 2.0 %collective-permute-done.3 = f32[128,512]{1,0:T(8,128)S(1)} collective-permute-done((f32[128,512]{1,0:T(8,128)S(1)}, f32[128,512]{1,0:T(8,128)S(1)}, u32[]{:S(2)}, u32[]{:S(2)}) %collective-permute-start.3) | collective-permute-done | bytes 262176 | tf_op jit(solution)/shard_map/ppermute | solution.py:59
  82.0 2.8 %collective-permute-done.4 = f32[128,512]{1,0:T(8,128)S(1)} collective-permute-done((f32[128,512]{1,0:T(8,128)S(1)}, f32[128,512]{1,0:T(8,128)S(1)}, u32[]{:S(2)}, u32[]{:S(2)}) %collective-permute-start.4) | collective-permute-done | bytes 262176 | tf_op jit(solution)/shard_map/ppermute | solution.py:59
  84.8 2.4 %convolution_add_fusion.1 = f32[128,512]{1,0:T(8,128)S(1)} fusion(f32[128,512]{1,0:T(8,128)S(1)} %fusion.4, f32[512,2048]{1,0:T(8,128)} %all-gather.3.cloned.1.call-done, f32[128,512]{1,0:T(8,128)S(1)} %collective-permute-done.3, f32[128,512]{1,0:T(8,128)S(1)} %collective-permute-done.4), kind=kOutput, calls=%fused_computation.6 | convolution fusion | flops 402784256 | bytes 2097152 | tf_op jit(solution)/shard_map/dot_general | solution.py:8
  87.3 2.4 %select_select_fusion.3 = (f32[128,512]{1,0:T(8,128)S(1)}, f32[128,512]{1,0:T(8,128)S(1)}) fusion(f32[128,512]{1,0:T(8,128)S(1)} %fusion.9, f32[128,512]{1,0:T(8,128)S(1)} %fusion.11, pred[]{:T(512)S(6)} %eq.71, pred[]{:T(512)S(6)} %eq.70, pred[]{:T(512)S(6)} %eq.69, f32[2048,512]{1,0:T(8,128)} %param.5, f32[128,512]{1,0:T(8,128)S(1)} %convolution_add_fusion.1, ...), kind=kOutput, calls=%fused_computation.24 | convolution fusion | flops 402915328 | bytes 2621443 | tf_op jit(solution)/shard_map/dot_general | solution.py:8
  89.7 0.7 collective-permute-start.5
  90.4 1.3 collective-permute-start.12
  91.7 1.3 collective-permute-start.13
  93.0 1.3 collective-permute-start.14
  94.4 0.0 collective-permute-done.5
  94.4 2.4 %fusion.1 = f32[128,512]{1,0:T(8,128)S(1)} fusion(f32[128,512]{1,0:T(8,128)S(1)} %convolution_add_fusion.1, f32[128,512]{1,0:T(8,128)S(1)} %collective-permute-done.5, f32[512,2048]{1,0:T(8,128)} %all-gather.3.cloned.1.call-done, f32[128,1024]{1,0:T(8,128)S(1)} %copy-done), kind=kOutput, calls=%fused_computation.5 | convolution fusion | flops 402784256 | bytes 2097152 | tf_op jit(solution)/shard_map/dot_general | solution.py:8
  96.8 2.4 %convolution_select_fusion = f32[128,512]{1,0:T(8,128)S(1)} fusion(f32[128,512]{1,0:T(8,128)S(1)} %get-tuple-element.17, f32[128,512]{1,0:T(8,128)S(1)} %fusion.1, f32[2048,512]{1,0:T(8,128)} %param.5, pred[]{:T(512)S(6)} %eq.68), kind=kOutput, calls=%fused_computation.3 | convolution fusion | flops 402718720 | bytes 1835009 | tf_op jit(solution)/shard_map/dot_general | solution.py:8
  99.2 0.7 collective-permute-start.6
  99.9 0.7 collective-permute-start.7
  100.5 0.0 collective-permute-done.12
  100.5 0.7 collective-permute-start.8
  101.2 0.0 collective-permute-done.13
  101.2 0.0 collective-permute-done.14
  101.3 0.1 select_select_fusion.1
  101.4 1.3 collective-permute-start.15
  102.7 1.3 collective-permute-start.16
  104.0 0.0 collective-permute-done.6
  104.0 1.3 collective-permute-start.17
  105.3 0.0 collective-permute-done.7
  105.3 0.0 collective-permute-done.8
  105.3 0.1 select_select_fusion.2
  105.4 0.7 collective-permute-start.10
  106.1 0.7 collective-permute-start.11
  106.8 0.0 collective-permute-done.15
  106.8 0.7 collective-permute-start.9
  107.5 1.0 collective-permute-done.16
  108.5 2.9 %collective-permute-done.17 = f32[128,512]{1,0:T(8,128)S(1)} collective-permute-done((f32[128,512]{1,0:T(8,128)S(1)}, f32[128,512]{1,0:T(8,128)S(1)}, u32[]{:S(2)}, u32[]{:S(2)}) %collective-permute-start.17) | collective-permute-done | bytes 262176 | tf_op jit(solution)/shard_map/ppermute | solution.py:70
  111.4 0.0 collective-permute-done.10
  111.4 0.0 collective-permute-done.11
  111.4 0.0 collective-permute-done.9
  111.4 0.2 select_select_fusion
  111.6 6.9 %collective-permute-start.18 = (f32[128,512]{1,0:T(8,128)S(1)}, f32[128,512]{1,0:T(8,128)S(1)}, u32[]{:S(2)}, u32[]{:S(2)}) collective-permute-start(f32[128,512]{1,0:T(8,128)S(1)} %select_select_fusion), channel_id=1, source_target_pairs={{0,8},{4,12},{8,0},{12,4},{16,24},{20,28},{24,16},{28,20},{32,40},... | collective-permute-start | bytes 786440 | tf_op jit(solution)/shard_map/ppermute | solution.py:77
  118.6 6.5 %collective-permute-done.18 = f32[128,512]{1,0:T(8,128)S(1)} collective-permute-done((f32[128,512]{1,0:T(8,128)S(1)}, f32[128,512]{1,0:T(8,128)S(1)}, u32[]{:S(2)}, u32[]{:S(2)}) %collective-permute-start.18) | collective-permute-done | bytes 262176 | tf_op jit(solution)/shard_map/ppermute | solution.py:77
  125.2 1.0 collective-permute-start.19
  126.2 1.5 %collective-permute-done.19 = f32[128,1024]{1,0:T(8,128)S(1)} collective-permute-done((f32[128,1024]{1,0:T(8,128)S(1)}, f32[128,1024]{1,0:T(8,128)S(1)}, u32[]{:S(2)}, u32[]{:S(2)}) %collective-permute-start.19) | collective-permute-done | bytes 524320 | tf_op jit(solution)/shard_map/ppermute | solution.py:81
  127.7 6.5 %fusion = f32[128,512]{1,0:T(8,128)S(1)} fusion(f32[128,512]{1,0:T(8,128)S(1)} %convolution_select_fusion, f32[512,2048]{1,0:T(8,128)} %all-gather.3.cloned.1.call-done, pred[]{:T(512)S(6)} %lt.61, f32[128,512]{1,0:T(8,128)S(1)} %get-tuple-element.16, f32[128,512]{1,0:T(8,128)S(1)} %get-tuple-element.14, f32[128,512]{1,0:T(8,128)S(1)} %get-tuple-element.15, ...), kind=kOutput, calls=%fused_computation.2 | convolution fusion | flops 1612578816 | bytes 6029314 | tf_op jit(solution)/shard_map/dot_general | solution.py:8
  134.2 0.0 all-gather.5.cloned.1.call-done
  134.3 6.5 %convolution_subtract_fusion = f32[128,512]{1,0:T(8,128)S(1)} fusion(f32[512,2048]{1,0:T(8,128)} %all-gather.5.cloned.1.call-done, f32[128,1024]{1,0:T(8,128)S(1)} %copy-done, f32[128,512]{1,0:T(8,128)S(1)} %get-tuple-element.16, f32[128,512]{1,0:T(8,128)S(1)} %get-tuple-element.14, f32[128,512]{1,0:T(8,128)S(1)} %get-tuple-element.15, ...), kind=kOutput, calls=%fused_computation | convolution fusion | flops 1612513280 | bytes 5767169 | tf_op jit(solution)/shard_map/dot_general | solution.py:8
  140.8 0.8 pad_maximum_fusion
  (3 shorter events, 0.1 us)
Async XLA Ops:
  6.5 9.5 %copy-start = (f32[128,1024]{1,0:T(8,128)S(1)}, f32[128,1024]{1,0:T(8,128)}, u32[]{:S(2)}) copy-start(f32[128,1024]{1,0:T(8,128)} %param.3) | copy-start | bytes 1572868
  6.5 61.2 %all-gather.3.cloned.1.call-start = ((), (), s32[]{:S(2)}) async-start(), calls=%async_computation | async-start | bytes 5242880 | tf_op jit(solution)/shard_map/all_gather | solution.py:38
  7.6 5.9 %collective-permute-start = (f32[128,512]{1,0:T(8,128)S(1)}, f32[128,512]{1,0:T(8,128)S(1)}, u32[]{:S(2)}, u32[]{:S(2)}) collective-permute-start(f32[128,512]{1,0:T(8,128)S(1)} %slice.46), channel_id=1, source_target_pairs={{0,12},{1,13},{2,14},{3,15}} | collective-permute-start | bytes 786440 | tf_op jit(solution)/shard_map/ppermute | solution.py:36
  8.3 5.2 %collective-permute-start.1 = (f32[128,512]{1,0:T(8,128)S(1)}, f32[128,512]{1,0:T(8,128)S(1)}, u32[]{:S(2)}, u32[]{:S(2)}) collective-permute-start(f32[128,512]{1,0:T(8,128)S(1)} %slice.46), channel_id=1, source_target_pairs={{0,8},{1,9},{2,10},{3,11}} | collective-permute-start | bytes 786440 | tf_op jit(solution)/shard_map/ppermute | solution.py:36
  8.9 7.0 %collective-permute-start.2 = (f32[128,512]{1,0:T(8,128)S(1)}, f32[128,512]{1,0:T(8,128)S(1)}, u32[]{:S(2)}, u32[]{:S(2)}) collective-permute-start(f32[128,512]{1,0:T(8,128)S(1)} %slice.46), channel_id=1, source_target_pairs={{0,4},{1,5},{2,6},{3,7}} | collective-permute-start | bytes 786440 | tf_op jit(solution)/shard_map/ppermute | solution.py:36
  16.1 118.1 %all-gather.5.cloned.1.call-start = ((), (), s32[]{:S(2)}) async-start(), calls=%async_computation.1 | async-start | bytes 5242880 | tf_op jit(solution)/shard_map/all_gather | solution.py:40
  74.9 7.1 %collective-permute-start.3 = (f32[128,512]{1,0:T(8,128)S(1)}, f32[128,512]{1,0:T(8,128)S(1)}, u32[]{:S(2)}, u32[]{:S(2)}) collective-permute-start(f32[128,512]{1,0:T(8,128)S(1)} %fusion.9), channel_id=1, source_target_pairs={{4,8},{5,9},{6,10},{7,11}} | collective-permute-start | bytes 786440 | tf_op jit(solution)/shard_map/ppermute | solution.py:59
  78.7 6.1 %collective-permute-start.4 = (f32[128,512]{1,0:T(8,128)S(1)}, f32[128,512]{1,0:T(8,128)S(1)}, u32[]{:S(2)}, u32[]{:S(2)}) collective-permute-start(f32[128,512]{1,0:T(8,128)S(1)} %fusion.9), channel_id=1, source_target_pairs={{4,12},{5,13},{6,14},{7,15}} | collective-permute-start | bytes 786440 | tf_op jit(solution)/shard_map/ppermute | solution.py:59
  89.7 4.7 %collective-permute-start.5 = (f32[128,512]{1,0:T(8,128)S(1)}, f32[128,512]{1,0:T(8,128)S(1)}, u32[]{:S(2)}, u32[]{:S(2)}) collective-permute-start(f32[128,512]{1,0:T(8,128)S(1)} %get-tuple-element.18), channel_id=1, source_target_pairs={{8,12},{9,13},{10,14},{11,15}} | collective-permute-start | bytes 786440 | tf_op jit(solution)/shard_map/ppermute | solution.py:59
  90.4 10.1 %collective-permute-start.12 = (f32[128,512]{1,0:T(8,128)S(1)}, f32[128,512]{1,0:T(8,128)S(1)}, u32[]{:S(2)}, u32[]{:S(2)}) collective-permute-start(f32[128,512]{1,0:T(8,128)S(1)} %get-tuple-element.17), channel_id=1, source_target_pairs={{0,192},{4,196},{8,200},{1,193},{5,197},{9,201},{2,194},{6,198},{1... | collective-permute-start | bytes 786440 | tf_op jit(solution)/shard_map/ppermute | solution.py:70
  91.7 9.5 %collective-permute-start.13 = (f32[128,512]{1,0:T(8,128)S(1)}, f32[128,512]{1,0:T(8,128)S(1)}, u32[]{:S(2)}, u32[]{:S(2)}) collective-permute-start(f32[128,512]{1,0:T(8,128)S(1)} %get-tuple-element.17), channel_id=1, source_target_pairs={{0,64},{4,68},{8,72},{1,65},{5,69},{9,73},{2,66},{6,70},{10,74},{3... | collective-permute-start | bytes 786440 | tf_op jit(solution)/shard_map/ppermute | solution.py:70
  93.0 8.2 %collective-permute-start.14 = (f32[128,512]{1,0:T(8,128)S(1)}, f32[128,512]{1,0:T(8,128)S(1)}, u32[]{:S(2)}, u32[]{:S(2)}) collective-permute-start(f32[128,512]{1,0:T(8,128)S(1)} %get-tuple-element.17), channel_id=1, source_target_pairs={{0,128},{4,132},{8,136},{1,129},{5,133},{9,137},{2,130},{6,134},{1... | collective-permute-start | bytes 786440 | tf_op jit(solution)/shard_map/ppermute | solution.py:70
  99.2 4.8 %collective-permute-start.6 = (f32[128,512]{1,0:T(8,128)S(1)}, f32[128,512]{1,0:T(8,128)S(1)}, u32[]{:S(2)}, u32[]{:S(2)}) collective-permute-start(f32[128,512]{1,0:T(8,128)S(1)} %convolution_select_fusion), channel_id=1, source_target_pairs={{12,204},{13,205},{14,206},{15,207}} | collective-permute-start | bytes 786440 | tf_op jit(solution)/shard_map/ppermute | solution.py:70
  99.9 5.5 %collective-permute-start.7 = (f32[128,512]{1,0:T(8,128)S(1)}, f32[128,512]{1,0:T(8,128)S(1)}, u32[]{:S(2)}, u32[]{:S(2)}) collective-permute-start(f32[128,512]{1,0:T(8,128)S(1)} %convolution_select_fusion), channel_id=1, source_target_pairs={{12,76},{13,77},{14,78},{15,79}} | collective-permute-start | bytes 786440 | tf_op jit(solution)/shard_map/ppermute | solution.py:70
  100.5 4.8 %collective-permute-start.8 = (f32[128,512]{1,0:T(8,128)S(1)}, f32[128,512]{1,0:T(8,128)S(1)}, u32[]{:S(2)}, u32[]{:S(2)}) collective-permute-start(f32[128,512]{1,0:T(8,128)S(1)} %convolution_select_fusion), channel_id=1, source_target_pairs={{12,140},{13,141},{14,142},{15,143}} | collective-permute-start | bytes 786440 | tf_op jit(solution)/shard_map/ppermute | solution.py:70
  101.4 5.4 %collective-permute-start.15 = (f32[128,512]{1,0:T(8,128)S(1)}, f32[128,512]{1,0:T(8,128)S(1)}, u32[]{:S(2)}, u32[]{:S(2)}) collective-permute-start(f32[128,512]{1,0:T(8,128)S(1)} %select_select_fusion.1), channel_id=1, source_target_pairs={{0,48},{4,52},{8,56},{64,112},{68,116},{72,120},{128,176},{132,180... | collective-permute-start | bytes 786440 | tf_op jit(solution)/shard_map/ppermute | solution.py:70
  102.7 5.9 %collective-permute-start.16 = (f32[128,512]{1,0:T(8,128)S(1)}, f32[128,512]{1,0:T(8,128)S(1)}, u32[]{:S(2)}, u32[]{:S(2)}) collective-permute-start(f32[128,512]{1,0:T(8,128)S(1)} %select_select_fusion.1), channel_id=1, source_target_pairs={{0,16},{4,20},{8,24},{64,80},{68,84},{72,88},{128,144},{132,148},{... | collective-permute-start | bytes 786440 | tf_op jit(solution)/shard_map/ppermute | solution.py:70
  104.0 7.4 %collective-permute-start.17 = (f32[128,512]{1,0:T(8,128)S(1)}, f32[128,512]{1,0:T(8,128)S(1)}, u32[]{:S(2)}, u32[]{:S(2)}) collective-permute-start(f32[128,512]{1,0:T(8,128)S(1)} %select_select_fusion.1), channel_id=1, source_target_pairs={{0,32},{4,36},{8,40},{64,96},{68,100},{72,104},{128,160},{132,164}... | collective-permute-start | bytes 786440 | tf_op jit(solution)/shard_map/ppermute | solution.py:70
  105.4 5.9 %collective-permute-start.10 = (f32[128,512]{1,0:T(8,128)S(1)}, f32[128,512]{1,0:T(8,128)S(1)}, u32[]{:S(2)}, u32[]{:S(2)}) collective-permute-start(f32[128,512]{1,0:T(8,128)S(1)} %select_select_fusion.2), channel_id=1, source_target_pairs={{12,28},{76,92},{140,156},{204,220},{13,29},{77,93},{141,157},{205... | collective-permute-start | bytes 786440 | tf_op jit(solution)/shard_map/ppermute | solution.py:70
  106.1 5.3 %collective-permute-start.11 = (f32[128,512]{1,0:T(8,128)S(1)}, f32[128,512]{1,0:T(8,128)S(1)}, u32[]{:S(2)}, u32[]{:S(2)}) collective-permute-start(f32[128,512]{1,0:T(8,128)S(1)} %select_select_fusion.2), channel_id=1, source_target_pairs={{12,44},{76,108},{140,172},{204,236},{13,45},{77,109},{141,173},{2... | collective-permute-start | bytes 786440 | tf_op jit(solution)/shard_map/ppermute | solution.py:70
  106.8 4.6 %collective-permute-start.9 = (f32[128,512]{1,0:T(8,128)S(1)}, f32[128,512]{1,0:T(8,128)S(1)}, u32[]{:S(2)}, u32[]{:S(2)}) collective-permute-start(f32[128,512]{1,0:T(8,128)S(1)} %select_select_fusion.2), channel_id=1, source_target_pairs={{12,60},{76,124},{140,188},{204,252},{13,61},{77,125},{141,189},{2... | collective-permute-start | bytes 786440 | tf_op jit(solution)/shard_map/ppermute | solution.py:70
  111.6 13.5 %collective-permute-start.18 = (f32[128,512]{1,0:T(8,128)S(1)}, f32[128,512]{1,0:T(8,128)S(1)}, u32[]{:S(2)}, u32[]{:S(2)}) collective-permute-start(f32[128,512]{1,0:T(8,128)S(1)} %select_select_fusion), channel_id=1, source_target_pairs={{0,8},{4,12},{8,0},{12,4},{16,24},{20,28},{24,16},{28,20},{32,40},... | collective-permute-start | bytes 786440 | tf_op jit(solution)/shard_map/ppermute | solution.py:77
  125.2 2.5 %collective-permute-start.19 = (f32[128,1024]{1,0:T(8,128)S(1)}, f32[128,1024]{1,0:T(8,128)S(1)}, u32[]{:S(2)}, u32[]{:S(2)}) collective-permute-start(f32[128,1024]{1,0:T(8,128)S(1)} %maximum_select_fusion.1), channel_id=1, source_target_pairs={{0,4},{4,0},{8,12},{12,8},{16,20},{20,16},{24,28},{28,24},{32,36},... | collective-permute-start | bytes 1572872 | tf_op jit(solution)/shard_map/ppermute | solution.py:81
Sparse Core Ops, SparseCore 0:
  16.2 51.4 all-gather.2
  69.5 51.1 all-gather.4
where the time goes:
time: 149 us; the launch traced here: 148 us
  waiting for transfers between devices  70.9 us (48%)
  matrix products  29.8 us (20%)
  starting transfers between devices  28.3 us (19%)
  between operations  13.8 us (9%)
  local copies, waits for them, and re-layouts  4.28 us (3%)
    all_gather x1, waiting for transfers between devices, per_device(): lower_first = lax.all_gather(first_rows, 'pcol', axis=1, tiled=True)  51.6 us
    dot_general x9, matrix products, contract(): lax.dot_general(left, right, (((1,), (1,)), ((), ())), precision=lax.Prec...  29.8 us
    ppermute x12, starting transfers between devices, per_device(): arrived = lax.ppermute(piece, 'prow', pairs)  11.9 us
    ppermute x1, starting transfers between devices, per_device(): other = lax.ppermute(piece, 'prow', [(p, p ^ 2) for p in range(n_row)])  6.93 us
    ppermute x1, waiting for transfers between devices, per_device(): other = lax.ppermute(piece, 'prow', [(p, p ^ 2) for p in range(n_row)])  6.55 us
    ppermute x3, starting transfers between devices, per_device(): arrived = arrived + lax.ppermute(solved, AXES, pairs)  5.78 us
    ppermute x3, waiting for transfers between devices, per_device(): arrived = arrived + lax.ppermute(solved, AXES, pairs)  4.78 us
    ppermute x12, waiting for transfers between devices, per_device(): arrived = lax.ppermute(piece, 'prow', pairs)  3.86 us
  transfers between devices with their start and end apart: 22, of which 8 were waited for; matrix products, arithmetic and copies ran while one was open for 18% of the time, Pallas kernels for 0%

commit v1 on v0

--- a/solution.py
+++ b/solution.py
@@ -35,7 +35,12 @@
         pairs = [(at(0, c), at(i, c)) for c in range(n_col)]
         first_rhs = jnp.where(row_at == i, lax.ppermute(top_rhs, AXES, pairs), first_rhs)
     first_rhs, first_rows = lax.optimization_barrier((first_rhs, factor[:block]))
-    lower_first = lax.all_gather(first_rows, "pcol", axis=1, tiled=True)
+    lower_first = jnp.concatenate(
+        jax.lax.all_to_all(
+            jnp.stack([first_rows for _ in range(jax.lax.axis_size("pcol"))], axis=0), "pcol", 0, 0
+        ),
+        axis=1,
+    )
     second_rows, _ = lax.optimization_barrier((factor[block:], lower_first))
     lower_second = lax.all_gather(second_rows, "pcol", axis=1, tiled=True)
     acc = jnp.zeros((rhs_width, block), jnp.float32)

time: 149 us -> 148 us (level)
  waiting for transfers between devices: 70.9 us -> 17.6 us
  blocking collectives: 0 us -> 49.6 us
  starting transfers between devices: 28.3 us -> 33.5 us
  matrix products: 29.8 us -> 26.6 us
    all_gather x1 -> x0, waiting for transfers between devices: 51.6 us -> none  [per_device(): lower_first = lax.all_gather(first_rows, 'pcol', axis=1, tiled=True)]
    all_to_all x0 -> x1, blocking collectives: none -> 49.6 us  [per_device(): jax.lax.all_to_all(jnp.stack([first_rows for _ in range(jax.lax.axis_size...]
    ppermute x3, starting transfers between devices: 5.78 us -> 9.8 us  [per_device(): arrived = arrived + lax.ppermute(solved, AXES, pairs)]
    dot_general x9, matrix products: 29.8 us -> 26.6 us  [contract(): lax.dot_general(left, right, (((1,), (1,)), ((), ())), precision=lax.Prec...]
    ppermute x1, starting transfers between devices: 6.93 us -> 8.92 us  [per_device(): other = lax.ppermute(piece, 'prow', [(p, p ^ 2) for p in range(n_row)])]
  transfers between devices with their start and end apart: 22 -> 21, of which waited for: 8 -> 6; matrix products, arithmetic and copies ran while one was open for 18% -> 16% of each run, Pallas kernels for 0% -> 0%
where the time goes in v1:
time: 148 us; the launch traced here: 147 us
  blocking collectives  49.6 us (34%)
  starting transfers between devices  33.5 us (23%)
  matrix products  26.6 us (18%)
  waiting for transfers between devices  17.6 us (12%)
  between operations  13.9 us (9%)
  local copies, waits for them, and re-layouts  4.74 us (3%)
    all_to_all x1, blocking collectives, per_device(): jax.lax.all_to_all(jnp.stack([first_rows for _ in range(jax.lax.axis_size...  49.6 us
    dot_general x9, matrix products, contract(): lax.dot_general(left, right, (((1,), (1,)), ((), ())), precision=lax.Prec...  26.6 us
    ppermute x12, starting transfers between devices, per_device(): arrived = lax.ppermute(piece, 'prow', pairs)  11.9 us
    ppermute x3, starting transfers between devices, per_device(): arrived = arrived + lax.ppermute(solved, AXES, pairs)  9.8 us
    ppermute x1, starting transfers between devices, per_device(): other = lax.ppermute(piece, 'prow', [(p, p ^ 2) for p in range(n_row)])  8.92 us
    ppermute x1, waiting for transfers between devices, per_device(): other = lax.ppermute(piece, 'prow', [(p, p ^ 2) for p in range(n_row)])  5.39 us
    ppermute x3, waiting for transfers between devices, per_device(): arrived = arrived + lax.ppermute(solved, AXES, pairs)  4.78 us
  transfers between devices with their start and end apart: 21, of which 6 were waited for; matrix products, arithmetic and copies ran while one was open for 16% of the time, Pallas kernels for 0%

profile of v1, /device:TPU:1, one launch (start us, length us, event | category | flops | bytes accessed | tf_op | source)
XLA Modules:
  0.0 147.3 jit_solution(13922081473330476234)
XLA Ops:
  6.5 0.0 copy-start
  6.5 0.0 all-gather.2.cloned.1.call-start
  6.5 1.0 slice.46
  7.6 0.7 collective-permute-start
  8.3 0.7 collective-permute-start.1
  8.9 1.3 collective-permute-start.2
  10.3 2.8 %fusion.20 = (f32[512,512]{1,0:T(8,128)S(1)}, f32[512,512]{1,0:T(8,128)}) fusion(f32[1024,512]{1,0:T(8,128)} %param.4), kind=kLoop, calls=%fused_computation.33 | loop fusion | bytes 4194304 | tf_op jit(solution)/shard_map/slice | solution.py:37
  13.0 0.0 collective-permute-done
  13.0 0.0 collective-permute-done.1
  13.1 2.9 %collective-permute-done.2 = f32[128,512]{1,0:T(8,128)S(1)} collective-permute-done((f32[128,512]{1,0:T(8,128)S(1)}, f32[128,512]{1,0:T(8,128)S(1)}, u32[]{:S(2)}, u32[]{:S(2)}) %collective-permute-start.2) | collective-permute-done | bytes 262176 | tf_op jit(solution)/shard_map/ppermute | solution.py:36
  16.0 0.0 copy-done
  16.0 0.1 select_select_fusion.4
  16.1 0.3 copy.4
  16.4 0.5 stack.2
  16.9 49.6 %all_to_all.5 = f32[4,512,512]{1,2,0:T(8,128)} all-to-all(f32[4,512,512]{1,2,0:T(8,128)S(1)} %stack.2), channel_id=1, replica_groups=mesh['prow'=64,'pcol'=4] {'pcol'}, dimensions={0} | all-to-all | bytes 8388608 | tf_op jit(solution)/shard_map/all_to_all | solution.py:39
  66.5 0.0 all-gather.2.cloned.1.call-update
  66.6 2.4 %fusion.11 = f32[128,512]{1,0:T(8,128)S(1)} fusion(f32[128,512]{1,0:T(8,128)S(1)} %select_select_fusion.4, f32[2048,512]{1,0:T(8,128)} %param.5), kind=kOutput, calls=%fused_computation.17 | convolution fusion | flops 402653184 | bytes 1572864 | tf_op jit(solution)/shard_map/dot_general | solution.py:8
  69.0 1.9 %fusion.4 = f32[128,512]{1,0:T(8,128)S(1)} fusion(f32[128,512]{1,0:T(8,128)S(1)} %fusion.11, f32[512,2048]{0,1:T(8,128)} %bitcast.9), kind=kOutput, calls=%fused_computation.9 | convolution fusion | flops 402653184 | bytes 1572864 | tf_op jit(solution)/shard_map/dot_general | solution.py:8
  70.9 2.4 %fusion.9 = f32[128,512]{1,0:T(8,128)S(1)} fusion(f32[2048,512]{1,0:T(8,128)} %param.5, f32[128,512]{1,0:T(8,128)S(1)} %fusion.4, f32[128,1024]{1,0:T(8,128)S(1)} %copy-done), kind=kOutput, calls=%fused_computation.15 | convolution fusion | flops 402718720 | bytes 1835008 | tf_op jit(solution)/shard_map/dot_general | solution.py:8
  73.3 7.8 %collective-permute-start.3 = (f32[128,512]{1,0:T(8,128)S(1)}, f32[128,512]{1,0:T(8,128)S(1)}, u32[]{:S(2)}, u32[]{:S(2)}) collective-permute-start(f32[128,512]{1,0:T(8,128)S(1)} %fusion.9), channel_id=1, source_target_pairs={{4,8},{5,9},{6,10},{7,11}} | collective-permute-start | bytes 786440 | tf_op jit(solution)/shard_map/ppermute | solution.py:64
  81.1 1.3 collective-permute-start.4
  82.4 2.0 %collective-permute-done.3 = f32[128,512]{1,0:T(8,128)S(1)} collective-permute-done((f32[128,512]{1,0:T(8,128)S(1)}, f32[128,512]{1,0:T(8,128)S(1)}, u32[]{:S(2)}, u32[]{:S(2)}) %collective-permute-start.3) | collective-permute-done | bytes 262176 | tf_op jit(solution)/shard_map/ppermute | solution.py:64
  84.4 2.8 %collective-permute-done.4 = f32[128,512]{1,0:T(8,128)S(1)} collective-permute-done((f32[128,512]{1,0:T(8,128)S(1)}, f32[128,512]{1,0:T(8,128)S(1)}, u32[]{:S(2)}, u32[]{:S(2)}) %collective-permute-start.4) | collective-permute-done | bytes 262176 | tf_op jit(solution)/shard_map/ppermute | solution.py:64
  87.2 1.9 %convolution_add_fusion.1 = f32[128,512]{1,0:T(8,128)S(1)} fusion(f32[128,512]{1,0:T(8,128)S(1)} %fusion.4, f32[512,2048]{0,1:T(8,128)} %bitcast.10, f32[128,512]{1,0:T(8,128)S(1)} %collective-permute-done.3, f32[128,512]{1,0:T(8,128)S(1)} %collective-permute-done.4), kind=kOutput, calls=%fused_computation.6 | convolution fusion | flops 402784256 | bytes 2097152 | tf_op jit(solution)/shard_map/dot_general | solution.py:8
  89.2 2.4 %select_select_fusion.3 = (f32[128,512]{1,0:T(8,128)S(1)}, f32[128,512]{1,0:T(8,128)S(1)}) fusion(f32[128,512]{1,0:T(8,128)S(1)} %fusion.9, f32[128,512]{1,0:T(8,128)S(1)} %fusion.11, pred[]{:T(512)S(6)} %eq.71, pred[]{:T(512)S(6)} %eq.70, pred[]{:T(512)S(6)} %eq.69, f32[2048,512]{1,0:T(8,128)} %param.5, f32[128,512]{1,0:T(8,128)S(1)} %convolution_add_fusion.1, ...), kind=kOutput, calls=%fused_computation.24 | convolution fusion | flops 402915328 | bytes 2621443 | tf_op jit(solution)/shard_map/dot_general | solution.py:8
  91.6 0.7 collective-permute-start.5
  92.3 1.3 collective-permute-start.12
  93.6 1.3 collective-permute-start.13
  95.0 1.3 collective-permute-start.14
  96.3 0.0 collective-permute-done.5
  96.3 1.9 %fusion.1 = f32[128,512]{1,0:T(8,128)S(1)} fusion(f32[128,512]{1,0:T(8,128)S(1)} %convolution_add_fusion.1, f32[128,512]{1,0:T(8,128)S(1)} %collective-permute-done.5, f32[512,2048]{0,1:T(8,128)} %bitcast.11, f32[128,1024]{1,0:T(8,128)S(1)} %copy-done), kind=kOutput, calls=%fused_computation.5 | convolution fusion | flops 402784256 | bytes 2097152 | tf_op jit(solution)/shard_map/dot_general | solution.py:8
  98.2 2.4 %convolution_select_fusion = f32[128,512]{1,0:T(8,128)S(1)} fusion(f32[128,512]{1,0:T(8,128)S(1)} %get-tuple-element.17, f32[128,512]{1,0:T(8,128)S(1)} %fusion.1, f32[2048,512]{1,0:T(8,128)} %param.5, pred[]{:T(512)S(6)} %eq.68), kind=kOutput, calls=%fused_computation.3 | convolution fusion | flops 402718720 | bytes 1835009 | tf_op jit(solution)/shard_map/dot_general | solution.py:8
  100.6 0.7 collective-permute-start.6
  101.3 0.7 collective-permute-start.7
  102.0 0.0 collective-permute-done.12
  102.0 0.7 collective-permute-start.8
  102.7 0.0 collective-permute-done.13
  102.7 0.0 collective-permute-done.14
  102.7 0.1 select_select_fusion.1
  102.8 1.3 collective-permute-start.15
  104.1 1.3 collective-permute-start.16
  105.4 0.0 collective-permute-done.6
  105.5 1.3 collective-permute-start.17
  106.8 0.0 collective-permute-done.7
  106.8 0.0 collective-permute-done.8
  106.8 0.1 select_select_fusion.2
  106.9 0.7 collective-permute-start.10
  107.6 0.7 collective-permute-start.11
  108.3 0.0 collective-permute-done.15
  108.3 0.7 collective-permute-start.9
  109.0 0.0 collective-permute-done.16
  109.0 2.6 %collective-permute-done.17 = f32[128,512]{1,0:T(8,128)S(1)} collective-permute-done((f32[128,512]{1,0:T(8,128)S(1)}, f32[128,512]{1,0:T(8,128)S(1)}, u32[]{:S(2)}, u32[]{:S(2)}) %collective-permute-start.17) | collective-permute-done | bytes 262176 | tf_op jit(solution)/shard_map/ppermute | solution.py:75
  111.6 0.0 collective-permute-done.10
  111.6 0.0 collective-permute-done.11
  111.6 0.0 collective-permute-done.9
  111.6 0.2 select_select_fusion
  111.8 8.9 %collective-permute-start.18 = (f32[128,512]{1,0:T(8,128)S(1)}, f32[128,512]{1,0:T(8,128)S(1)}, u32[]{:S(2)}, u32[]{:S(2)}) collective-permute-start(f32[128,512]{1,0:T(8,128)S(1)} %select_select_fusion), channel_id=1, source_target_pairs={{0,8},{4,12},{8,0},{12,4},{16,24},{20,28},{24,16},{28,20},{32,40},... | collective-permute-start | bytes 786440 | tf_op jit(solution)/shard_map/ppermute | solution.py:82
  120.8 5.4 %collective-permute-done.18 = f32[128,512]{1,0:T(8,128)S(1)} collective-permute-done((f32[128,512]{1,0:T(8,128)S(1)}, f32[128,512]{1,0:T(8,128)S(1)}, u32[]{:S(2)}, u32[]{:S(2)}) %collective-permute-start.18) | collective-permute-done | bytes 262176 | tf_op jit(solution)/shard_map/ppermute | solution.py:82
  126.2 0.3 collective-permute-start.19
  126.5 1.8 %collective-permute-done.19 = f32[128,1024]{1,0:T(8,128)S(1)} collective-permute-done((f32[128,1024]{1,0:T(8,128)S(1)}, f32[128,1024]{1,0:T(8,128)S(1)}, u32[]{:S(2)}, u32[]{:S(2)}) %collective-permute-start.19) | collective-permute-done | bytes 524320 | tf_op jit(solution)/shard_map/ppermute | solution.py:86
  128.4 4.6 %fusion = f32[128,512]{1,0:T(8,128)S(1)} fusion(f32[128,512]{1,0:T(8,128)S(1)} %convolution_select_fusion, f32[512,2048]{0,1:T(8,128)} %bitcast.12, pred[]{:T(512)S(6)} %lt.61, f32[128,512]{1,0:T(8,128)S(1)} %get-tuple-element.16, f32[128,512]{1,0:T(8,128)S(1)} %get-tuple-element.14, f32[128,512]{1,0:T(8,128)S(1)} %get-tuple-element.15, ...), kind=kOutput, calls=%fused_computation.2 | convolution fusion | flops 1612578816 | bytes 6029314 | tf_op jit(solution)/shard_map/dot_general | solution.py:8
  133.1 0.0 all-gather.2.cloned.1.call-done
  133.1 6.5 %convolution_subtract_fusion = f32[128,512]{1,0:T(8,128)S(1)} fusion(f32[512,2048]{1,0:T(8,128)} %all-gather.2.cloned.1.call-done, f32[128,1024]{1,0:T(8,128)S(1)} %copy-done, f32[128,512]{1,0:T(8,128)S(1)} %get-tuple-element.16, f32[128,512]{1,0:T(8,128)S(1)} %get-tuple-element.14, f32[128,512]{1,0:T(8,128)S(1)} %get-tuple-element.15, ...), kind=kOutput, calls=%fused_computation | convolution fusion | flops 1612513280 | bytes 5767169 | tf_op jit(solution)/shard_map/dot_general | solution.py:8
  139.6 0.8 pad_maximum_fusion
  (3 shorter events, 0.1 us)
Async XLA Ops:
  6.5 9.5 %copy-start = (f32[128,1024]{1,0:T(8,128)S(1)}, f32[128,1024]{1,0:T(8,128)}, u32[]{:S(2)}) copy-start(f32[128,1024]{1,0:T(8,128)} %param.3) | copy-start | bytes 1572868
  6.5 126.6 %all-gather.2.cloned.1.call-start = ((), (), s32[]{:S(2)}) async-start(), calls=%async_computation.1 | async-start | bytes 5242880 | tf_op jit(solution)/shard_map/all_gather | solution.py:45
  7.6 5.5 %collective-permute-start = (f32[128,512]{1,0:T(8,128)S(1)}, f32[128,512]{1,0:T(8,128)S(1)}, u32[]{:S(2)}, u32[]{:S(2)}) collective-permute-start(f32[128,512]{1,0:T(8,128)S(1)} %slice.46), channel_id=1, source_target_pairs={{0,12},{1,13},{2,14},{3,15}} | collective-permute-start | bytes 786440 | tf_op jit(solution)/shard_map/ppermute | solution.py:36
  8.3 4.8 %collective-permute-start.1 = (f32[128,512]{1,0:T(8,128)S(1)}, f32[128,512]{1,0:T(8,128)S(1)}, u32[]{:S(2)}, u32[]{:S(2)}) collective-permute-start(f32[128,512]{1,0:T(8,128)S(1)} %slice.46), channel_id=1, source_target_pairs={{0,8},{1,9},{2,10},{3,11}} | collective-permute-start | bytes 786440 | tf_op jit(solution)/shard_map/ppermute | solution.py:36
  8.9 7.0 %collective-permute-start.2 = (f32[128,512]{1,0:T(8,128)S(1)}, f32[128,512]{1,0:T(8,128)S(1)}, u32[]{:S(2)}, u32[]{:S(2)}) collective-permute-start(f32[128,512]{1,0:T(8,128)S(1)} %slice.46), channel_id=1, source_target_pairs={{0,4},{1,5},{2,6},{3,7}} | collective-permute-start | bytes 786440 | tf_op jit(solution)/shard_map/ppermute | solution.py:36
  73.3 11.1 %collective-permute-start.3 = (f32[128,512]{1,0:T(8,128)S(1)}, f32[128,512]{1,0:T(8,128)S(1)}, u32[]{:S(2)}, u32[]{:S(2)}) collective-permute-start(f32[128,512]{1,0:T(8,128)S(1)} %fusion.9), channel_id=1, source_target_pairs={{4,8},{5,9},{6,10},{7,11}} | collective-permute-start | bytes 786440 | tf_op jit(solution)/shard_map/ppermute | solution.py:64
  81.1 6.1 %collective-permute-start.4 = (f32[128,512]{1,0:T(8,128)S(1)}, f32[128,512]{1,0:T(8,128)S(1)}, u32[]{:S(2)}, u32[]{:S(2)}) collective-permute-start(f32[128,512]{1,0:T(8,128)S(1)} %fusion.9), channel_id=1, source_target_pairs={{4,12},{5,13},{6,14},{7,15}} | collective-permute-start | bytes 786440 | tf_op jit(solution)/shard_map/ppermute | solution.py:64
  91.6 4.7 %collective-permute-start.5 = (f32[128,512]{1,0:T(8,128)S(1)}, f32[128,512]{1,0:T(8,128)S(1)}, u32[]{:S(2)}, u32[]{:S(2)}) collective-permute-start(f32[128,512]{1,0:T(8,128)S(1)} %get-tuple-element.18), channel_id=1, source_target_pairs={{8,12},{9,13},{10,14},{11,15}} | collective-permute-start | bytes 786440 | tf_op jit(solution)/shard_map/ppermute | solution.py:64
  92.3 9.7 %collective-permute-start.12 = (f32[128,512]{1,0:T(8,128)S(1)}, f32[128,512]{1,0:T(8,128)S(1)}, u32[]{:S(2)}, u32[]{:S(2)}) collective-permute-start(f32[128,512]{1,0:T(8,128)S(1)} %get-tuple-element.17), channel_id=1, source_target_pairs={{0,192},{4,196},{8,200},{1,193},{5,197},{9,201},{2,194},{6,198},{1... | collective-permute-start | bytes 786440 | tf_op jit(solution)/shard_map/ppermute | solution.py:75
  93.6 9.1 %collective-permute-start.13 = (f32[128,512]{1,0:T(8,128)S(1)}, f32[128,512]{1,0:T(8,128)S(1)}, u32[]{:S(2)}, u32[]{:S(2)}) collective-permute-start(f32[128,512]{1,0:T(8,128)S(1)} %get-tuple-element.17), channel_id=1, source_target_pairs={{0,64},{4,68},{8,72},{1,65},{5,69},{9,73},{2,66},{6,70},{10,74},{3... | collective-permute-start | bytes 786440 | tf_op jit(solution)/shard_map/ppermute | solution.py:75
  95.0 7.8 %collective-permute-start.14 = (f32[128,512]{1,0:T(8,128)S(1)}, f32[128,512]{1,0:T(8,128)S(1)}, u32[]{:S(2)}, u32[]{:S(2)}) collective-permute-start(f32[128,512]{1,0:T(8,128)S(1)} %get-tuple-element.17), channel_id=1, source_target_pairs={{0,128},{4,132},{8,136},{1,129},{5,133},{9,137},{2,130},{6,134},{1... | collective-permute-start | bytes 786440 | tf_op jit(solution)/shard_map/ppermute | solution.py:75
  100.6 4.8 %collective-permute-start.6 = (f32[128,512]{1,0:T(8,128)S(1)}, f32[128,512]{1,0:T(8,128)S(1)}, u32[]{:S(2)}, u32[]{:S(2)}) collective-permute-start(f32[128,512]{1,0:T(8,128)S(1)} %convolution_select_fusion), channel_id=1, source_target_pairs={{12,204},{13,205},{14,206},{15,207}} | collective-permute-start | bytes 786440 | tf_op jit(solution)/shard_map/ppermute | solution.py:75
  101.3 5.5 %collective-permute-start.7 = (f32[128,512]{1,0:T(8,128)S(1)}, f32[128,512]{1,0:T(8,128)S(1)}, u32[]{:S(2)}, u32[]{:S(2)}) collective-permute-start(f32[128,512]{1,0:T(8,128)S(1)} %convolution_select_fusion), channel_id=1, source_target_pairs={{12,76},{13,77},{14,78},{15,79}} | collective-permute-start | bytes 786440 | tf_op jit(solution)/shard_map/ppermute | solution.py:75
  102.0 4.8 %collective-permute-start.8 = (f32[128,512]{1,0:T(8,128)S(1)}, f32[128,512]{1,0:T(8,128)S(1)}, u32[]{:S(2)}, u32[]{:S(2)}) collective-permute-start(f32[128,512]{1,0:T(8,128)S(1)} %convolution_select_fusion), channel_id=1, source_target_pairs={{12,140},{13,141},{14,142},{15,143}} | collective-permute-start | bytes 786440 | tf_op jit(solution)/shard_map/ppermute | solution.py:75
  102.8 5.4 %collective-permute-start.15 = (f32[128,512]{1,0:T(8,128)S(1)}, f32[128,512]{1,0:T(8,128)S(1)}, u32[]{:S(2)}, u32[]{:S(2)}) collective-permute-start(f32[128,512]{1,0:T(8,128)S(1)} %select_select_fusion.1), channel_id=1, source_target_pairs={{0,48},{4,52},{8,56},{64,112},{68,116},{72,120},{128,176},{132,180... | collective-permute-start | bytes 786440 | tf_op jit(solution)/shard_map/ppermute | solution.py:75
  104.1 4.9 %collective-permute-start.16 = (f32[128,512]{1,0:T(8,128)S(1)}, f32[128,512]{1,0:T(8,128)S(1)}, u32[]{:S(2)}, u32[]{:S(2)}) collective-permute-start(f32[128,512]{1,0:T(8,128)S(1)} %select_select_fusion.1), channel_id=1, source_target_pairs={{0,16},{4,20},{8,24},{64,80},{68,84},{72,88},{128,144},{132,148},{... | collective-permute-start | bytes 786440 | tf_op jit(solution)/shard_map/ppermute | solution.py:75
  105.5 6.1 %collective-permute-start.17 = (f32[128,512]{1,0:T(8,128)S(1)}, f32[128,512]{1,0:T(8,128)S(1)}, u32[]{:S(2)}, u32[]{:S(2)}) collective-permute-start(f32[128,512]{1,0:T(8,128)S(1)} %select_select_fusion.1), channel_id=1, source_target_pairs={{0,32},{4,36},{8,40},{64,96},{68,100},{72,104},{128,160},{132,164}... | collective-permute-start | bytes 786440 | tf_op jit(solution)/shard_map/ppermute | solution.py:75
  106.9 4.7 %collective-permute-start.10 = (f32[128,512]{1,0:T(8,128)S(1)}, f32[128,512]{1,0:T(8,128)S(1)}, u32[]{:S(2)}, u32[]{:S(2)}) collective-permute-start(f32[128,512]{1,0:T(8,128)S(1)} %select_select_fusion.2), channel_id=1, source_target_pairs={{12,28},{76,92},{140,156},{204,220},{13,29},{77,93},{141,157},{205... | collective-permute-start | bytes 786440 | tf_op jit(solution)/shard_map/ppermute | solution.py:75
  107.6 4.0 %collective-permute-start.11 = (f32[128,512]{1,0:T(8,128)S(1)}, f32[128,512]{1,0:T(8,128)S(1)}, u32[]{:S(2)}, u32[]{:S(2)}) collective-permute-start(f32[128,512]{1,0:T(8,128)S(1)} %select_select_fusion.2), channel_id=1, source_target_pairs={{12,44},{76,108},{140,172},{204,236},{13,45},{77,109},{141,173},{2... | collective-permute-start | bytes 786440 | tf_op jit(solution)/shard_map/ppermute | solution.py:75
  108.3 3.3 %collective-permute-start.9 = (f32[128,512]{1,0:T(8,128)S(1)}, f32[128,512]{1,0:T(8,128)S(1)}, u32[]{:S(2)}, u32[]{:S(2)}) collective-permute-start(f32[128,512]{1,0:T(8,128)S(1)} %select_select_fusion.2), channel_id=1, source_target_pairs={{12,60},{76,124},{140,188},{204,252},{13,61},{77,125},{141,189},{2... | collective-permute-start | bytes 786440 | tf_op jit(solution)/shard_map/ppermute | solution.py:75
  111.8 14.3 %collective-permute-start.18 = (f32[128,512]{1,0:T(8,128)S(1)}, f32[128,512]{1,0:T(8,128)S(1)}, u32[]{:S(2)}, u32[]{:S(2)}) collective-permute-start(f32[128,512]{1,0:T(8,128)S(1)} %select_select_fusion), channel_id=1, source_target_pairs={{0,8},{4,12},{8,0},{12,4},{16,24},{20,28},{24,16},{28,20},{32,40},... | collective-permute-start | bytes 786440 | tf_op jit(solution)/shard_map/ppermute | solution.py:82
  126.2 2.2 %collective-permute-start.19 = (f32[128,1024]{1,0:T(8,128)S(1)}, f32[128,1024]{1,0:T(8,128)S(1)}, u32[]{:S(2)}, u32[]{:S(2)}) collective-permute-start(f32[128,1024]{1,0:T(8,128)S(1)} %maximum_select_fusion.1), channel_id=1, source_target_pairs={{0,4},{4,0},{8,12},{12,8},{16,20},{20,16},{24,28},{28,24},{32,36},... | collective-permute-start | bytes 1572872 | tf_op jit(solution)/shard_map/ppermute | solution.py:86
Sparse Core Ops, SparseCore 0:
  66.7 52.6 all-gather.1
